TPU v7x, 256 devices: a whole 4x4x8 slice. The times are simulated.
256 devices in a mesh: section: 16 (over y, x_hi, core), expert: 16 (over x_lo, z).
Axes of the slice: x: 4 (x_hi: 2, x_lo: 2; x = x_hi * 2 + x_lo), y: 4, z: 8, core: 2. Of those that a mesh axis runs over, the one named last changes fastest.
Arguments:
- tokens: bfloat16 [16, 2048, 7168], P('section', 'expert'), may hold values from -6 to 6
- cotangent: bfloat16 [16, 2048, 7168], P('section', 'expert'), may hold values from -6 to 6
- expert_ids: int32 [16, 2048, 8], P('section', 'expert'), may hold values from 0 to 31, as said below
- slot_index: int32 [16, 2048, 8], P('section', 'expert'), may hold values from 0 to 31, as said below
- gate_scale: float32 [16, 2048, 8], P('section', 'expert'), may hold values from 0.2 to 1.2
- gate_weight: bfloat16 [16, 7168, 2048], P('section', None, 'expert'), may hold values from -0.0625 to 0.0625
- up_weight: bfloat16 [16, 7168, 2048], P('section', None, 'expert'), may hold values from -0.0625 to 0.0625
- down_weight: bfloat16 [16, 2048, 7168], P('section', 'expert'), may hold values from -0.125 to 0.125
Outputs:
- next_input: bfloat16 [16, 2048, 7168], P('section', 'expert')
- prior_grad: bfloat16 [16, 2048, 7168], P('section', 'expert')
Inputs may be any that keep to these rules, and one draw needn't show every extreme that they name: `expert_ids`: each token names 8 different experts; among the 128 tokens of one device every expert is named exactly 32 times. `slot_index`: among the routes of one device's tokens to one expert, the slots are 0 to 31, each once.
All inputs are finite; a program needn't handle non-finite values.
Results may differ from a plain program's by a relative error of at most 0.011.
Values may be sent and summed in bfloat16 or wider, within the bound.
No kernel may reach another device: no remote copies, remote signals or barrier semaphores. Data moves between devices by JAX's collectives and lax.ppermute only.
A program may use at most 128 MiB of HBM per device.

v0:
```python
import jax
import jax.numpy as jnp
from jax import lax
from jax.sharding import PartitionSpec as P

CAP = 32


def from_behind(x, axis, by):
    length = lax.axis_size(axis)
    pairs = [(i, i + by) for i in range(length) if 0 <= i + by < length]
    return lax.ppermute(x, axis, pairs)


def silu_parts(gate):
    sig = jax.nn.sigmoid(gate)
    return (gate * sig, sig * (1.0 + gate * (1.0 - sig)))


def body(
    tokens, cotangent, expert_ids, slot_index, gate_scale, gate_weight, up_weight, down_weight
):
    section = lax.axis_index("section")
    local = tokens[0]
    grad_out = cotangent[0]
    named = expert_ids[0]
    gate_mat = gate_weight[0]
    up_mat = up_weight[0]
    down_mat = down_weight[0]
    width_local = gate_mat.shape[1]
    hit = named == section
    chosen = jnp.any(hit, axis=1)
    slot = jnp.sum(jnp.where(hit, slot_index[0], 0), axis=1)
    weight = jnp.sum(jnp.where(hit, gate_scale[0], jnp.float32(0.0)), axis=1)
    places = jnp.arange(CAP, dtype=jnp.int32)
    table = ((places[:, None] == slot[None, :]) & chosen[None, :]).astype(jnp.bfloat16)
    sent = jnp.dot(table, local, preferred_element_type=jnp.float32).astype(jnp.bfloat16)
    carried = (weight[:, None] * grad_out.astype(jnp.float32)).astype(jnp.bfloat16)
    back = jnp.dot(table, carried, preferred_element_type=jnp.float32).astype(jnp.bfloat16)
    piece = lax.all_gather(sent, "expert", axis=0, tiled=True)
    gate_up = jnp.concatenate(
        [
            jnp.dot(piece, gate_mat, preferred_element_type=jnp.float32),
            jnp.dot(piece, up_mat, preferred_element_type=jnp.float32),
        ],
        axis=1,
    )
    gate = gate_up[:, :width_local]
    up = gate_up[:, width_local:]
    act, slope = silu_parts(gate)
    hidden = (act * up).astype(jnp.bfloat16)
    combined = lax.psum_scatter(
        jnp.dot(hidden, down_mat, preferred_element_type=jnp.float32).astype(jnp.bfloat16),
        "expert",
        scatter_dimension=0,
        tiled=True,
    ).astype(jnp.float32)
    grad_hidden = jnp.dot(
        lax.all_gather(back, "expert", axis=0, tiled=True),
        down_mat.T,
        preferred_element_type=jnp.float32,
    )
    grad_up = (grad_hidden * act).astype(jnp.bfloat16)
    grad_gate = (grad_hidden * up * slope).astype(jnp.bfloat16)
    behind = jnp.dot(grad_gate, gate_mat.T, preferred_element_type=jnp.float32)
    inward = lax.psum_scatter(
        (behind + jnp.dot(grad_up, up_mat.T, preferred_element_type=jnp.float32)).astype(
            jnp.bfloat16
        ),
        "expert",
        scatter_dimension=0,
        tiled=True,
    ).astype(jnp.float32)
    output = local.astype(jnp.float32) + weight[:, None] * jnp.take(combined, slot, axis=0)
    grad_in = grad_out.astype(jnp.float32) + jnp.where(
        chosen[:, None], jnp.take(inward, slot, axis=0), jnp.float32(0.0)
    )
    next_input = from_behind(output.astype(jnp.bfloat16)[None], "section", 1)
    prior_grad = from_behind(grad_in.astype(jnp.bfloat16)[None], "section", -1)
    return (next_input, prior_grad)


def solution(mesh):
    in_specs = (
        P("section", "expert", None),
        P("section", "expert", None),
        P("section", "expert", None),
        P("section", "expert", None),
        P("section", "expert", None),
        P("section", None, "expert"),
        P("section", None, "expert"),
        P("section", "expert", None),
    )
    out_specs = (P("section", "expert", None), P("section", "expert", None))
    return jax.shard_map(body, mesh=mesh, in_specs=in_specs, out_specs=out_specs, check_vma=False)
```

profile of v0, /device:TPU:1, one launch (start us, length us, event | category | flops | bytes accessed | tf_op | source)
XLA Modules:
  0.0 467.2 jit_solution(15120559337887811934)
XLA Ops:
  7.2 0.0 copy-start
  7.2 0.0 all-gather.3.cloned.1.call-start
  7.2 0.8 select_reduce_fusion.1
  8.1 0.7 select_reduce_fusion
  8.8 2.6 convolution_convert_fusion.2
  11.4 0.0 all-gather.3.cloned.1.call-update
  11.5 0.0 all-gather.5.cloned.1.call-start
  11.5 2.8 convolution_convert_fusion.1
  14.3 0.0 all-gather.5.cloned.1.call-update
  14.3 0.0 reduce-scatter.5.cloned.1.call-start
  14.4 91.3 %all-gather.3.cloned.1.call-done = bf16[512,7168]{1,0:T(8,128)(2,1)} async-done(((bf16[32,7168]{1,0:T(8,128)(2,1)}), bf16[512,7168]{1,0:T(8,128)(2,1)}) %all-gather.3.cloned.1.call-update) | async-done | bytes 7340048 | tf_op jit(solution)/shard_map/all_gather | solution.py:40
  105.6 0.0 copy-done
  105.6 0.0 copy-start.2
  105.6 0.0 copy-start.5
  105.6 5.3 %fusion.16 = f32[512,128]{1,0:T(8,128)S(1)} fusion(bf16[512,7168]{1,0:T(8,128)(2,1)} %all-gather.3.cloned.1.call-done, bf16[1,7168,128]{2,1,0:T(8,128)(2,1)S(1)} %copy-done), kind=kOutput, calls=%fused_computation.25 | convolution fusion | flops 939524096 | bytes 9437184 | tf_op jit(solution)/shard_map/dot_general | solution.py:43
  110.9 0.0 copy-done.2
  110.9 0.4 copy-done.5
  111.4 2.1 fusion.12
  113.4 82.7 %all-gather.5.cloned.1.call-done = bf16[512,7168]{1,0:T(8,128)(2,1)} async-done(((bf16[32,7168]{1,0:T(8,128)(2,1)}), bf16[512,7168]{1,0:T(8,128)(2,1)}) %all-gather.5.cloned.1.call-update) | async-done | bytes 7340048 | tf_op jit(solution)/shard_map/all_gather | solution.py:59
  196.1 5.6 %fusion.8 = f32[512,128]{1,0:T(8,128)S(1)} fusion(bf16[512,7168]{1,0:T(8,128)(2,1)} %all-gather.5.cloned.1.call-done, bf16[1,128,7168]{2,1,0:T(8,128)(2,1)} %param.17), kind=kOutput, calls=%fused_computation.17 | convolution fusion | flops 939524096 | bytes 9437184 | tf_op jit(solution)/shard_map/dot_general | solution.py:58
  201.8 0.0 copy-start.3
  201.8 7.3 %fusion.14 = f32[512,7168]{1,0:T(8,128)} fusion(bf16[1,7168,128]{2,1,0:T(8,128)(2,1)S(1)} %copy-done, f32[512,128]{1,0:T(8,128)S(1)} %fusion.16, f32[512,128]{1,0:T(8,128)S(1)} %fusion.8, f32[512,128]{1,0:T(8,128)S(1)} %fusion.12), kind=kOutput, calls=%fused_computation.23 | convolution fusion | flops 940179456 | bytes 17301504 | tf_op jit(solution)/shard_map/dot_general | solution.py:65
  209.1 0.0 copy-done.3
  209.1 10.2 %add_convert_fusion = bf16[512,7168]{1,0:T(8,128)(2,1)} fusion(f32[512,7168]{1,0:T(8,128)} %fusion.14, bf16[1,7168,128]{2,1,0:T(8,128)(2,1)S(1)} %copy-done.3, f32[512,128]{1,0:T(8,128)S(1)} %fusion.8, f32[512,128]{1,0:T(8,128)S(1)} %fusion.16), kind=kOutput, calls=%fused_computation.2 | convolution fusion | flops 947257344 | bytes 24379392 | tf_op jit(solution)/shard_map/dot_general | solution.py:67
  219.3 0.0 copy-start.4
  219.3 0.0 reduce-scatter.5.cloned.1.call-update
  219.3 0.2 reduce-scatter.3.cloned.1.call-start
  219.5 1.2 copy-done.4
  220.8 5.0 %convolution_convert_fusion = bf16[512,7168]{1,0:T(8,128)(2,1)} fusion(bf16[1,128,7168]{2,1,0:T(8,128)(2,1)S(1)} %copy-done.4, f32[512,128]{1,0:T(8,128)S(1)} %fusion.12, f32[512,128]{1,0:T(8,128)S(1)} %fusion.16), kind=kOutput, calls=%fused_computation.3 | convolution fusion | flops 943587328 | bytes 9699328 | tf_op jit(solution)/shard_map/dot_general | solution.py:53
  225.8 0.0 reduce-scatter.3.cloned.1.call-update
  225.9 80.5 %reduce-scatter.5.cloned.1.call-done = bf16[32,7168]{1,0:T(8,128)(2,1)} async-done(((bf16[512,7168]{1,0:T(8,128)(2,1)}), bf16[32,7168]{1,0:T(8,128)(2,1)}) %reduce-scatter.5.cloned.1.call-update) | async-done | bytes 458768 | tf_op jit(solution)/shard_map/reduce_scatter | solution.py:66
  306.3 1.1 convert_element_type.60
  307.4 3.6 gather_fusion.1
  311.0 87.2 %reduce-scatter.3.cloned.1.call-done = bf16[32,7168]{1,0:T(8,128)(2,1)} async-done(((bf16[512,7168]{1,0:T(8,128)(2,1)}), bf16[32,7168]{1,0:T(8,128)(2,1)}) %reduce-scatter.3.cloned.1.call-update) | async-done | bytes 458768 | tf_op jit(solution)/shard_map/reduce_scatter | solution.py:52
  398.2 1.1 convert_element_type.51
  399.2 3.4 gather_fusion
  402.7 5.7 %fusion.5 = (bf16[1,128,7168]{2,1,0:T(8,128)(2,1)S(1)}, bf16[1,128,7168]{2,1,0:T(8,128)(2,1)S(1)}) fusion(f32[128,7168]{1,0:T(8,128)} %gather_fusion.1, bf16[1,128,7168]{2,1,0:T(8,128)(2,1)} %param.11, pred[128]{0:T(512)(128)(4,1)S(1)} %compare_and_fusion, pred[128]{0:T(512)(128)(4,1)S(1)} %reduce_or.9, f32[128,7168]{1,0:T(8,128)} %gather_fusion, ...), kind=kLoop, calls=%fused_computation.15 | loop fusion | flops 9175040 | bytes 14680832 | tf_op jit(solution)/shard_map/broadcast_in_dim | solution.py:79
  408.4 8.2 %collective-permute-start = (bf16[1,128,7168]{2,1,0:T(8,128)(2,1)S(1)}, bf16[1,128,7168]{2,1,0:T(8,128)(2,1)S(1)}, u32[]{:S(2)}, u32[]{:S(2)}) collective-permute-start(bf16[1,128,7168]{2,1,0:T(8,128)(2,1)S(1)} %get-tuple-element.6), channel_id=1, source_target_pairs={{0,16},{16,32},{32,48},{48,64},{64,80},{80,96},{96,112},{112,128},... | collective-permute-start | bytes 5505032 | tf_op jit(solution)/shard_map/ppermute | solution.py:12
  416.6 0.0 copy-start.1
  416.6 2.1 collective-permute-start.1
  418.6 18.1 %collective-permute-done = bf16[1,128,7168]{2,1,0:T(8,128)(2,1)S(1)} collective-permute-done((bf16[1,128,7168]{2,1,0:T(8,128)(2,1)S(1)}, bf16[1,128,7168]{2,1,0:T(8,128)(2,1)S(1)}, u32[]{:S(2)}, u32[]{:S(2)}) %collective-permute-start) | collective-permute-done | bytes 1835040 | tf_op jit(solution)/shard_map/ppermute | solution.py:12
  436.7 21.5 %collective-permute-done.1 = bf16[1,128,7168]{2,1,0:T(8,128)(2,1)S(1)} collective-permute-done((bf16[1,128,7168]{2,1,0:T(8,128)(2,1)S(1)}, bf16[1,128,7168]{2,1,0:T(8,128)(2,1)S(1)}, u32[]{:S(2)}, u32[]{:S(2)}) %collective-permute-start.1) | collective-permute-done | bytes 1835040 | tf_op jit(solution)/shard_map/ppermute | solution.py:12
  458.2 1.2 copy.12
  459.5 1.2 copy.13
  460.7 0.0 copy-done.1
  (4 shorter events, 0.0 us)
Async XLA Ops:
  7.2 98.5 %copy-start = (bf16[1,7168,128]{2,1,0:T(8,128)(2,1)S(1)}, bf16[1,7168,128]{2,1,0:T(8,128)(2,1)}, u32[]{:S(2)}) copy-start(bf16[1,7168,128]{2,1,0:T(8,128)(2,1)} %param.15) | copy-start | bytes 5505028
  7.2 98.5 %all-gather.3.cloned.1.call-start = ((), (), s32[]{:S(2)}) async-start(), calls=%async_computation.2 | async-start | bytes 7798784 | tf_op jit(solution)/shard_map/all_gather | solution.py:40
  11.5 184.7 %all-gather.5.cloned.1.call-start = ((), (), s32[]{:S(2)}) async-start(), calls=%async_computation.4 | async-start | bytes 7798784 | tf_op jit(solution)/shard_map/all_gather | solution.py:59
  14.3 292.0 %reduce-scatter.5.cloned.1.call-start = ((), (), s32[]{:S(2)}) async-start(), calls=%async_computation.5 | async-start | bytes 7798784 | tf_op jit(solution)/shard_map/reduce_scatter | solution.py:66
  105.6 5.3 %copy-start.2 = (bf16[1,7168,128]{2,1,0:T(8,128)(2,1)S(1)}, bf16[1,7168,128]{2,1,0:T(8,128)(2,1)}, u32[]{:S(2)}) copy-start(bf16[1,7168,128]{2,1,0:T(8,128)(2,1)} %param.16) | copy-start | bytes 5505028
  105.6 5.7 %copy-start.5 = (bf16[512,7168]{1,0:T(8,128)(2,1)S(1)}, bf16[512,7168]{1,0:T(8,128)(2,1)}, u32[]{:S(2)}) copy-start(bf16[512,7168]{1,0:T(8,128)(2,1)} %all-gather.3.cloned.1.call-done) | copy-start | bytes 22020100
  201.8 7.3 %copy-start.3 = (bf16[1,7168,128]{2,1,0:T(8,128)(2,1)S(1)}, bf16[1,7168,128]{2,1,0:T(8,128)(2,1)}, u32[]{:S(2)}) copy-start(bf16[1,7168,128]{2,1,0:T(8,128)(2,1)} %param.16) | copy-start | bytes 5505028
  219.3 1.5 copy-start.4
  219.3 178.9 %reduce-scatter.3.cloned.1.call-start = ((), (), s32[]{:S(2)}) async-start(), calls=%async_computation.3 | async-start | bytes 7798784 | tf_op jit(solution)/shard_map/reduce_scatter | solution.py:52
  408.4 28.3 %collective-permute-start = (bf16[1,128,7168]{2,1,0:T(8,128)(2,1)S(1)}, bf16[1,128,7168]{2,1,0:T(8,128)(2,1)S(1)}, u32[]{:S(2)}, u32[]{:S(2)}) collective-permute-start(bf16[1,128,7168]{2,1,0:T(8,128)(2,1)S(1)} %get-tuple-element.6), channel_id=1, source_target_pairs={{0,16},{16,32},{32,48},{48,64},{64,80},{80,96},{96,112},{112,128},... | collective-permute-start | bytes 5505032 | tf_op jit(solution)/shard_map/ppermute | solution.py:12
  416.6 44.1 %copy-start.1 = (bf16[1,7168,128]{2,1,0:T(8,128)(2,1)S(1)}, bf16[1,7168,128]{2,1,0:T(8,128)(2,1)}, u32[]{:S(2)}) copy-start(bf16[1,7168,128]{2,1,0:T(8,128)(2,1)} %param.15) | copy-start | bytes 5505028
  416.6 41.7 %collective-permute-start.1 = (bf16[1,128,7168]{2,1,0:T(8,128)(2,1)S(1)}, bf16[1,128,7168]{2,1,0:T(8,128)(2,1)S(1)}, u32[]{:S(2)}, u32[]{:S(2)}) collective-permute-start(bf16[1,128,7168]{2,1,0:T(8,128)(2,1)S(1)} %get-tuple-element.5), channel_id=1, source_target_pairs={{16,0},{32,16},{48,32},{64,48},{80,64},{96,80},{112,96},{128,112},... | collective-permute-start | bytes 5505032 | tf_op jit(solution)/shard_map/ppermute | solution.py:12
Sparse Core Ops, SparseCore 0:
  11.6 94.0 all-gather.2
  108.0 88.0 all-gather.4
  219.4 86.8 reduce-scatter.4
  308.7 89.3 reduce-scatter.2
where the time goes:
time: 468 us; the launch traced here: 467 us
  waiting for transfers between devices  381 us (81%)
  matrix products  40.9 us (9%)
  between operations  13.9 us (3%)
  local copies, waits for them, and re-layouts  11.2 us (2%)
  starting transfers between devices  10.6 us (2%)
  other arithmetic  9.46 us (2%)
    all_gather x1, waiting for transfers between devices, body(): piece = lax.all_gather(sent, 'expert', axis=0, tiled=True)  91.3 us
    reduce_scatter x1, waiting for transfers between devices, body(): lax.psum_scatter(jnp.dot(hidden, down_mat, preferred_element_type=jnp.flo...  87.2 us
    all_gather x1, waiting for transfers between devices, body(): lax.all_gather(back, 'expert', axis=0, tiled=True)  82.7 us
    reduce_scatter x1, waiting for transfers between devices, body(): lax.psum_scatter((behind + jnp.dot(grad_up, up_mat.T, preferred_element_t...  80.5 us
    ppermute x2, waiting for transfers between devices, from_behind(): return lax.ppermute(x, axis, pairs)  39.6 us
    ppermute x2, starting transfers between devices, from_behind(): return lax.ppermute(x, axis, pairs)  10.2 us
    dot_general x1, matrix products, body(): jnp.dot(grad_up, up_mat.T, preferred_element_type=jnp.float32)  10.2 us
  transfers between devices with their start and end apart: 6, of which 6 were waited for; matrix products, arithmetic and copies ran while one was open for 4% of the time, Pallas kernels for 0%

commit v1 on v0

--- a/solution.py
+++ b/solution.py
@@ -1,9 +1,20 @@
+import functools
 import jax
 import jax.numpy as jnp
 from jax import lax
 from jax.sharding import PartitionSpec as P
 
 CAP = 32
+
+
+def bench_keep_up(matrix, d_out):
+    return jnp.concatenate(
+        lax.all_to_all(jnp.stack(lax.axis_size("expert") * [matrix], axis=0), "expert", 0, 0),
+        axis=d_out,
+    )
+
+
+terms_get = functools.partial(bench_keep_up, d_out=0)
 
 
 def from_behind(x, axis, by):
@@ -55,11 +66,7 @@
         scatter_dimension=0,
         tiled=True,
     ).astype(jnp.float32)
-    grad_hidden = jnp.dot(
-        lax.all_gather(back, "expert", axis=0, tiled=True),
-        down_mat.T,
-        preferred_element_type=jnp.float32,
-    )
+    grad_hidden = jnp.dot(terms_get(back), down_mat.T, preferred_element_type=jnp.float32)
     grad_up = (grad_hidden * act).astype(jnp.bfloat16)
     grad_gate = (grad_hidden * up * slope).astype(jnp.bfloat16)
     behind = jnp.dot(grad_gate, gate_mat.T, preferred_element_type=jnp.float32)

time: 468 us -> 536 us (1.15)
  waiting for transfers between devices: 381 us -> 436 us
  starting transfers between devices: 10.6 us -> 21.1 us
    all_to_all x0 -> x1, waiting for transfers between devices: none -> 210 us  [bench_keep_up(): lax.all_to_all(jnp.stack(lax.axis_size('expert') * [matrix], axis=0), 'ex...]
    all_gather x1 -> x0, waiting for transfers between devices: 82.7 us -> none  [body(): lax.all_gather(back, 'expert', axis=0, tiled=True)]
    all_gather x1, waiting for transfers between devices: 91.3 us -> 18.2 us  [body(): piece = lax.all_gather(sent, 'expert', axis=0, tiled=True)]
    all_to_all x0 -> x1, starting transfers between devices: none -> 10.1 us  [bench_keep_up(): lax.all_to_all(jnp.stack(lax.axis_size('expert') * [matrix], axis=0), 'ex...]
  transfers between devices with their start and end apart: 6 -> 6, of which waited for: 6 -> 6; matrix products, arithmetic and copies ran while one was open for 4% -> 3% of each run, Pallas kernels for 0% -> 0%
where the time goes in v1:
time: 536 us
  waiting for transfers between devices  436 us (81%)
  matrix products  40.2 us (8%)
  starting transfers between devices  21.1 us (4%)
  local copies, waits for them, and re-layouts  15 us (3%)
  between operations  13.9 us (3%)
  other arithmetic  9.46 us (2%)
    all_to_all x1, waiting for transfers between devices, bench_keep_up(): lax.all_to_all(jnp.stack(lax.axis_size('expert') * [matrix], axis=0), 'ex...  210 us
    reduce_scatter x1, waiting for transfers between devices, body(): lax.psum_scatter(jnp.dot(hidden, down_mat, preferred_element_type=jnp.flo...  87.4 us
    reduce_scatter x1, waiting for transfers between devices, body(): lax.psum_scatter((behind + jnp.dot(grad_up, up_mat.T, preferred_element_t...  80.8 us
    ppermute x2, waiting for transfers between devices, from_behind(): return lax.ppermute(x, axis, pairs)  39.7 us
    all_gather x1, waiting for transfers between devices, body(): piece = lax.all_gather(sent, 'expert', axis=0, tiled=True)  18.2 us
    ppermute x2, starting transfers between devices, from_behind(): return lax.ppermute(x, axis, pairs)  10.8 us
  transfers between devices with their start and end apart: 6, of which 6 were waited for; matrix products, arithmetic and copies ran while one was open for 3% of the time, Pallas kernels for 0%

profile of v1, /device:TPU:1, one launch (start us, length us, event | category | flops | bytes accessed | tf_op | source)
XLA Modules:
  0.0 535.7 jit_solution(5500474076872119954)
XLA Ops:
  7.2 0.0 copy-start
  7.2 0.9 select_reduce_fusion.1
  8.0 0.7 select_reduce_fusion
  8.8 2.0 convolution_convert_fusion.1
  10.8 3.8 stack.2
  14.6 10.1 %all-to-all-start = ((bf16[16,32,7168]{2,1,0:T(8,128)(2,1)}), bf16[16,32,7168]{2,1,0:T(8,128)(2,1)}, u32[]{:S(2)}, u32[]{:S(2)}) async-start(bf16[16,32,7168]{2,1,0:T(8,128)(2,1)} %stack.2), calls=%async_computation.1 | async-start | bytes 14680064 | tf_op jit(solution)/shard_map/all_to_all | solution.py:12
  24.7 0.0 all-gather.2.cloned.1.call-start
  24.7 2.6 convolution_convert_fusion.2
  27.4 0.0 all-gather.2.cloned.1.call-update
  27.4 0.0 reduce-scatter.5.cloned.1.call-start
  27.4 210.0 %all-to-all-done = bf16[16,32,7168]{2,1,0:T(8,128)(2,1)} async-done(((bf16[16,32,7168]{2,1,0:T(8,128)(2,1)}), bf16[16,32,7168]{2,1,0:T(8,128)(2,1)}, u32[]{:S(2)}, u32[]{:S(2)}) %all-to-all-start) | async-done | bytes 7340064 | tf_op jit(solution)/shard_map/all_to_all | solution.py:12
  237.4 5.7 %fusion.8 = f32[512,128]{1,0:T(8,128)S(1)} fusion(bf16[512,7168]{1,0:T(8,128)(2,1)} %bitcast.7, bf16[1,128,7168]{2,1,0:T(8,128)(2,1)} %param.17), kind=kOutput, calls=%fused_computation.17 | convolution fusion | flops 939524096 | bytes 9437184 | tf_op jit(solution)/shard_map/dot_general | solution.py:69
  243.1 18.2 %all-gather.2.cloned.1.call-done = bf16[512,7168]{1,0:T(8,128)(2,1)} async-done(((bf16[32,7168]{1,0:T(8,128)(2,1)}), bf16[512,7168]{1,0:T(8,128)(2,1)}) %all-gather.2.cloned.1.call-update) | async-done | bytes 7340048 | tf_op jit(solution)/shard_map/all_gather | solution.py:51
  261.3 0.0 copy-done
  261.3 0.0 copy-start.2
  261.3 0.0 copy-start.4
  261.3 5.3 fusion.16
  266.6 0.0 copy-done.2
  266.6 0.4 copy-done.4
  267.0 2.1 fusion.12
  269.1 7.3 %fusion.14 = f32[512,7168]{1,0:T(8,128)} fusion(bf16[1,7168,128]{2,1,0:T(8,128)(2,1)S(1)} %copy-done, f32[512,128]{1,0:T(8,128)S(1)} %fusion.16, f32[512,128]{1,0:T(8,128)S(1)} %fusion.8, f32[512,128]{1,0:T(8,128)S(1)} %fusion.12), kind=kOutput, calls=%fused_computation.23 | convolution fusion | flops 940179456 | bytes 17301504 | tf_op jit(solution)/shard_map/dot_general | solution.py:72
  276.4 10.2 %add_convert_fusion = bf16[512,7168]{1,0:T(8,128)(2,1)} fusion(f32[512,7168]{1,0:T(8,128)} %fusion.14, bf16[1,7168,128]{2,1,0:T(8,128)(2,1)S(1)} %copy-done.2, f32[512,128]{1,0:T(8,128)S(1)} %fusion.8, f32[512,128]{1,0:T(8,128)S(1)} %fusion.16), kind=kOutput, calls=%fused_computation.2 | convolution fusion | flops 947257344 | bytes 24379392 | tf_op jit(solution)/shard_map/dot_general | solution.py:74
  286.5 0.0 copy-start.3
  286.5 0.0 reduce-scatter.5.cloned.1.call-update
  286.6 0.2 reduce-scatter.3.cloned.1.call-start
  286.8 1.2 copy-done.3
  288.0 5.0 convolution_convert_fusion
  293.1 0.0 reduce-scatter.3.cloned.1.call-update
  293.1 80.8 %reduce-scatter.5.cloned.1.call-done = bf16[32,7168]{1,0:T(8,128)(2,1)} async-done(((bf16[512,7168]{1,0:T(8,128)(2,1)}), bf16[32,7168]{1,0:T(8,128)(2,1)}) %reduce-scatter.5.cloned.1.call-update) | async-done | bytes 458768 | tf_op jit(solution)/shard_map/reduce_scatter | solution.py:73
  374.0 1.1 convert_element_type.60
  375.1 3.6 gather_fusion.1
  378.6 87.4 %reduce-scatter.3.cloned.1.call-done = bf16[32,7168]{1,0:T(8,128)(2,1)} async-done(((bf16[512,7168]{1,0:T(8,128)(2,1)}), bf16[32,7168]{1,0:T(8,128)(2,1)}) %reduce-scatter.3.cloned.1.call-update) | async-done | bytes 458768 | tf_op jit(solution)/shard_map/reduce_scatter | solution.py:63
  466.0 1.1 convert_element_type.51
  467.1 3.4 gather_fusion
  470.5 5.7 %fusion.5 = (bf16[1,128,7168]{2,1,0:T(8,128)(2,1)S(1)}, bf16[1,128,7168]{2,1,0:T(8,128)(2,1)S(1)}) fusion(f32[128,7168]{1,0:T(8,128)} %gather_fusion.1, bf16[1,128,7168]{2,1,0:T(8,128)(2,1)} %param.11, pred[128]{0:T(512)(128)(4,1)S(1)} %compare_and_fusion, pred[128]{0:T(512)(128)(4,1)S(1)} %reduce_or.9, f32[128,7168]{1,0:T(8,128)} %gather_fusion, ...), kind=kLoop, calls=%fused_computation.15 | loop fusion | flops 9175040 | bytes 14680832 | tf_op jit(solution)/shard_map/broadcast_in_dim | solution.py:86
  476.2 8.7 %collective-permute-start = (bf16[1,128,7168]{2,1,0:T(8,128)(2,1)S(1)}, bf16[1,128,7168]{2,1,0:T(8,128)(2,1)S(1)}, u32[]{:S(2)}, u32[]{:S(2)}) collective-permute-start(bf16[1,128,7168]{2,1,0:T(8,128)(2,1)S(1)} %get-tuple-element.6), channel_id=1, source_target_pairs={{0,16},{16,32},{32,48},{48,64},{64,80},{80,96},{96,112},{112,128},... | collective-permute-start | bytes 5505032 | tf_op jit(solution)/shard_map/ppermute | solution.py:23
  484.9 0.0 copy-start.1
  485.0 2.1 collective-permute-start.1
  487.0 18.1 %collective-permute-done = bf16[1,128,7168]{2,1,0:T(8,128)(2,1)S(1)} collective-permute-done((bf16[1,128,7168]{2,1,0:T(8,128)(2,1)S(1)}, bf16[1,128,7168]{2,1,0:T(8,128)(2,1)S(1)}, u32[]{:S(2)}, u32[]{:S(2)}) %collective-permute-start) | collective-permute-done | bytes 1835040 | tf_op jit(solution)/shard_map/ppermute | solution.py:23
  505.1 21.6 %collective-permute-done.1 = bf16[1,128,7168]{2,1,0:T(8,128)(2,1)S(1)} collective-permute-done((bf16[1,128,7168]{2,1,0:T(8,128)(2,1)S(1)}, bf16[1,128,7168]{2,1,0:T(8,128)(2,1)S(1)}, u32[]{:S(2)}, u32[]{:S(2)}) %collective-permute-start.1) | collective-permute-done | bytes 1835040 | tf_op jit(solution)/shard_map/ppermute | solution.py:23
  526.7 1.2 copy.12
  527.9 1.2 copy.13
  529.2 0.0 copy-done.1
  (4 shorter events, 0.0 us)
Async XLA Ops:
  7.2 254.1 %copy-start = (bf16[1,7168,128]{2,1,0:T(8,128)(2,1)S(1)}, bf16[1,7168,128]{2,1,0:T(8,128)(2,1)}, u32[]{:S(2)}) copy-start(bf16[1,7168,128]{2,1,0:T(8,128)(2,1)} %param.15) | copy-start | bytes 5505028
  14.6 222.8 %all-to-all-start = ((bf16[16,32,7168]{2,1,0:T(8,128)(2,1)}), bf16[16,32,7168]{2,1,0:T(8,128)(2,1)}, u32[]{:S(2)}, u32[]{:S(2)}) async-start(bf16[16,32,7168]{2,1,0:T(8,128)(2,1)} %stack.2), calls=%async_computation.1 | async-start | bytes 14680064 | tf_op jit(solution)/shard_map/all_to_all | solution.py:12
  24.7 236.6 %all-gather.2.cloned.1.call-start = ((), (), s32[]{:S(2)}) async-start(), calls=%async_computation.3 | async-start | bytes 7798784 | tf_op jit(solution)/shard_map/all_gather | solution.py:51
  27.4 346.6 %reduce-scatter.5.cloned.1.call-start = ((), (), s32[]{:S(2)}) async-start(), calls=%async_computation.5 | async-start | bytes 7798784 | tf_op jit(solution)/shard_map/reduce_scatter | solution.py:73
  261.3 5.3 copy-start.2
  261.3 5.7 %copy-start.4 = (bf16[512,7168]{1,0:T(8,128)(2,1)S(1)}, bf16[512,7168]{1,0:T(8,128)(2,1)}, u32[]{:S(2)}) copy-start(bf16[512,7168]{1,0:T(8,128)(2,1)} %all-gather.2.cloned.1.call-done) | copy-start | bytes 22020100
  286.5 1.5 copy-start.3
  286.6 179.4 %reduce-scatter.3.cloned.1.call-start = ((), (), s32[]{:S(2)}) async-start(), calls=%async_computation.4 | async-start | bytes 7798784 | tf_op jit(solution)/shard_map/reduce_scatter | solution.py:63
  476.2 28.9 %collective-permute-start = (bf16[1,128,7168]{2,1,0:T(8,128)(2,1)S(1)}, bf16[1,128,7168]{2,1,0:T(8,128)(2,1)S(1)}, u32[]{:S(2)}, u32[]{:S(2)}) collective-permute-start(bf16[1,128,7168]{2,1,0:T(8,128)(2,1)S(1)} %get-tuple-element.6), channel_id=1, source_target_pairs={{0,16},{16,32},{32,48},{48,64},{64,80},{80,96},{96,112},{112,128},... | collective-permute-start | bytes 5505032 | tf_op jit(solution)/shard_map/ppermute | solution.py:23
  484.9 44.2 %copy-start.1 = (bf16[1,7168,128]{2,1,0:T(8,128)(2,1)S(1)}, bf16[1,7168,128]{2,1,0:T(8,128)(2,1)}, u32[]{:S(2)}) copy-start(bf16[1,7168,128]{2,1,0:T(8,128)(2,1)} %param.15) | copy-start | bytes 5505028
  485.0 41.7 %collective-permute-start.1 = (bf16[1,128,7168]{2,1,0:T(8,128)(2,1)S(1)}, bf16[1,128,7168]{2,1,0:T(8,128)(2,1)S(1)}, u32[]{:S(2)}, u32[]{:S(2)}) collective-permute-start(bf16[1,128,7168]{2,1,0:T(8,128)(2,1)S(1)} %get-tuple-element.5), channel_id=1, source_target_pairs={{16,0},{32,16},{48,32},{64,48},{80,64},{96,80},{112,96},{128,112},... | collective-permute-start | bytes 5505032 | tf_op jit(solution)/shard_map/ppermute | solution.py:23
Sparse Core Ops, SparseCore 0:
  27.8 233.3 all-gather.1
  286.7 87.2 reduce-scatter.4
  376.5 89.3 reduce-scatter.2
